TPU v7x, 128 devices: a whole 4x4x4 slice. The times are simulated.
128 devices in a mesh: seq: 16 (over y, x_lo, core), tp: 8 (over z, x_hi).
Axes of the slice: x: 4 (x_hi: 2, x_lo: 2; x = x_hi * 2 + x_lo), y: 4, z: 4, core: 2. Of those that a mesh axis runs over, the one named last changes fastest.
Arguments:
- tokens: bfloat16 [8192, 4096], P('seq'), may hold values from -6 to 6
- norm_gain: bfloat16 [4096], replicated, may hold values from 0.099609375 to 1.8984375
- w_query: bfloat16 [4096, 4096], P(None, 'tp'), may hold values from -4 to 4
- w_key: bfloat16 [4096, 512], replicated, may hold values from -1 to 1
- w_value: bfloat16 [4096, 512], replicated, may hold values from -0.09375 to 0.09375
- w_out: bfloat16 [4096, 4096], P('tp'), may hold values from -0.375 to 0.375
- prompt_lengths: int32 [16], replicated, may hold values from 1 to 6144, 8192 in all
- page_slots: int32 [64], replicated, may hold values from 0 to 63, each once
Outputs:
- attended: bfloat16 [8192, 4096], P(('seq', 'tp'))
- kv_cache: bfloat16 [64, 128, 1024], P('seq', None, 'tp')
Inputs may be any that keep to these rules, and one draw needn't show every extreme that they name: `prompt_lengths`: the lengths sum to 8192; the longest prompt has exactly 6144 tokens. `page_slots`: every value appears exactly once.
All inputs are finite; a program needn't handle non-finite values.
Results may differ from a plain program's by a relative error of at most 0.015.
Values may be sent and summed in bfloat16 or wider, within the bound.
No kernel may reach another device: no remote copies, remote signals or barrier semaphores. Data moves between devices by JAX's collectives and lax.ppermute only.
A program may use at most 128 MiB of HBM per device.

v0:
```python
import jax
import jax.numpy as jnp
from jax import lax
from jax.sharding import PartitionSpec as P

HD = 128
PAGE = 128
epsilon = 1e-05
rope_base = 5000000.0


def segment_info(token_index, prompt_lengths):
    prompt_ends = jnp.cumsum(prompt_lengths)
    finished = prompt_ends[None, :] <= token_index[:, None]
    segment = jnp.sum(finished.astype(jnp.int32), axis=1)
    offset = jnp.sum(jnp.where(finished, prompt_lengths[None, :], 0), axis=1)
    return (segment, token_index - offset)


def rotate(vectors, position):
    half_size = HD // 2
    frequency = rope_base ** (-(2.0 * jnp.arange(half_size, dtype=jnp.float32)) / HD)
    angle = position.astype(jnp.float32)[:, None] * frequency[None, :]
    cosine = jnp.cos(angle)[:, None, :]
    sine = jnp.sin(angle)[:, None, :]
    first_half = vectors[..., :half_size]
    second_half = vectors[..., half_size:]
    return jnp.concatenate(
        [first_half * cosine - second_half * sine, second_half * cosine + first_half * sine],
        axis=-1,
    )


def normalize(tokens, norm_gain):
    hidden = tokens.astype(jnp.float32)
    factor = lax.rsqrt(jnp.mean(hidden * hidden, axis=-1, keepdims=True) + epsilon)
    return (hidden * factor * norm_gain.astype(jnp.float32)).astype(jnp.bfloat16)


def attend(
    head_state,
    group_queries,
    group_index,
    group_segment,
    key_rows,
    value_rows,
    key_index,
    key_segment,
):
    running_max, running_sum, weighted = head_state
    scores = jnp.einsum(
        "rhd,nd->hrn", group_queries, key_rows, preferred_element_type=jnp.float32
    ) * HD ** (-0.5)
    visible = (
        (key_index[None, :] <= group_index[:, None])
        & (key_segment[None, :] == group_segment[:, None])
    )[None]
    fresh_max = jnp.maximum(running_max, jnp.max(jnp.where(visible, scores, -1e30), axis=2))
    weights = jnp.where(visible, jnp.exp(scores - fresh_max[..., None]), 0.0)
    shrink = jnp.exp(running_max - fresh_max)
    running_sum = running_sum * shrink + jnp.sum(weights, axis=2)
    weighted = weighted * shrink[..., None] + jnp.einsum(
        "hrn,nd->hrd", weights.astype(jnp.bfloat16), value_rows, preferred_element_type=jnp.float32
    )
    return (fresh_max, running_sum, weighted)


def on_device(tokens, norm_gain, w_query, w_key, w_value, w_out, prompt_lengths, page_slots):
    row_count = tokens.shape[0]
    tp_count = lax.axis_size("tp")
    seq_rank = lax.axis_index("seq")
    tp_rank = lax.axis_index("tp")
    heads_here = w_query.shape[1] // HD
    kv_heads = w_key.shape[1] // HD
    sharing = tp_count // kv_heads
    kv_head = tp_rank // sharing
    token_index = seq_rank * row_count + jnp.arange(row_count, dtype=jnp.int32)
    segment, position = segment_info(token_index, prompt_lengths)
    normed = normalize(tokens, norm_gain)
    queries = rotate(
        jnp.dot(normed, w_query, preferred_element_type=jnp.float32).reshape(
            row_count, heads_here, HD
        ),
        position,
    ).astype(jnp.bfloat16)
    key_columns = lax.dynamic_slice_in_dim(w_key, kv_head * HD, HD, 1)
    value_columns = lax.dynamic_slice_in_dim(w_value, kv_head * HD, HD, 1)
    keys_here = rotate(
        jnp.dot(normed, key_columns, preferred_element_type=jnp.float32)[:, None, :], position
    )[:, 0].astype(jnp.bfloat16)
    values_here = jnp.dot(normed, value_columns, preferred_element_type=jnp.float32).astype(
        jnp.bfloat16
    )
    keys_values = jnp.concatenate([keys_here, values_here], axis=1)
    cache_width = 2 * HD // sharing
    cache_column = tp_rank % sharing * cache_width
    slots_here = row_count // PAGE
    cache_rows = jnp.arange(slots_here * PAGE, dtype=jnp.int32)
    page_total = page_slots.shape[0]
    groups = ((queries, token_index, segment),)

    def step_block(carried, block_input):
        states, cache_here = carried
        block_values, block_start = block_input
        block_size = block_values.shape[0]
        key_index = block_start + jnp.arange(block_size, dtype=jnp.int32)
        key_segment, unused_key_position = segment_info(key_index, prompt_lengths)
        key_rows = block_values[:, :HD]
        value_rows = block_values[:, HD:]
        updated = []
        for head_state, group in zip(states, groups):
            group_queries, group_index, group_segment = group
            head_state = attend(
                head_state,
                group_queries,
                group_index,
                group_segment,
                key_rows,
                value_rows,
                key_index,
                key_segment,
            )
            updated.append(head_state)
        page_number = key_index // PAGE
        global_slot = jnp.sum(
            jnp.where(
                page_number[:, None] == jnp.arange(page_total, dtype=jnp.int32)[None, :],
                page_slots[None, :],
                0,
            ),
            axis=1,
        )
        cache_target = jnp.where(
            global_slot // slots_here == seq_rank,
            global_slot % slots_here * PAGE + key_index % PAGE,
            -1,
        )
        selector = (cache_rows[:, None] == cache_target[None, :]).astype(jnp.bfloat16)
        page_part = lax.dynamic_slice_in_dim(block_values, cache_column, cache_width, 1)
        cache_here = cache_here + jnp.dot(
            selector, page_part, preferred_element_type=jnp.float32
        ).astype(jnp.bfloat16)
        return ((tuple(updated), cache_here), None)

    initial_states = tuple(
        (
            (
                jnp.full((heads_here, group[1].shape[0]), -1e30, jnp.float32),
                jnp.zeros((heads_here, group[1].shape[0]), jnp.float32),
                jnp.zeros((heads_here, group[1].shape[0], HD), jnp.float32),
            )
            for group in groups
        )
    )
    initial_cache = jnp.zeros((slots_here * PAGE, cache_width), jnp.bfloat16)
    carried = (initial_states, initial_cache)
    shard_piece = lax.all_gather(keys_values, "seq", axis=0, tiled=True)
    piece_rows = shard_piece.shape[0]
    block_rows = 512
    blocks = shard_piece.reshape(piece_rows // block_rows, block_rows, 2 * HD)
    block_starts = block_rows * jnp.arange(piece_rows // block_rows, dtype=jnp.int32)
    carried, unused_output = lax.scan(step_block, carried, (blocks, block_starts))
    states, cache_here = carried
    outputs = [
        (weighted / running_sum[..., None])
        .transpose(1, 0, 2)
        .reshape(-1, heads_here * HD)
        .astype(jnp.bfloat16)
        for running_max, running_sum, weighted in states
    ]
    heads_out = outputs[0]
    attended = lax.psum_scatter(
        jnp.dot(heads_out, w_out, preferred_element_type=jnp.float32).astype(jnp.bfloat16),
        "tp",
        scatter_dimension=0,
        tiled=True,
    )
    return (attended, cache_here.reshape(slots_here, PAGE, cache_width))


def solution(mesh):
    placed = (P("seq", None), P(), P(None, "tp"), P(), P(), P("tp", None), P(), P())
    return jax.shard_map(
        on_device,
        mesh=mesh,
        in_specs=placed,
        out_specs=(P(("seq", "tp"), None), P("seq", None, "tp")),
        check_vma=False,
    )
```

profile of v0, /device:TPU:0, one launch (start us, length us, event | category | flops | bytes accessed | tf_op | source)
XLA Modules:
  0.0 305.7 jit_solution(4409422071376044708)
XLA Ops:
  8.1 3.1 %fusion.33 = f32[512]{0:T(512)S(1)} fusion(bf16[512,4096]{1,0:T(8,128)(2,1)} %param.10), kind=kLoop, calls=%fused_computation.59 | loop fusion | flops 6290944 | bytes 4196352 | tf_op jit(solution)/shard_map/reduce_sum | solution.py:36
  11.4 4.2 %convolution_convert_fusion.2 = bf16[512,128]{0,1:T(8,128)(2,1)S(1)} fusion(bf16[4096,512]{1,0:T(8,128)(2,1)} %param.14, s32[]{:T(128)S(6)} %select_n.116, bf16[512,4096]{1,0:T(8,128)(2,1)} %param.10, f32[4096]{0:T(1024)S(1)} %convert_element_type.64, f32[512]{0:T(512)S(1)} %add_rsqrt_fusion), kind=kOutput, calls=%fused_computation.64 | convolution fusion | flops 545325056 | bytes 5392388 | tf_op jit(solution)/shard_map/dot_general | solution.py:91
  15.6 2.8 convolution_bitcast_fusion
  20.1 5.9 %fusion.50 = f32[512,512]{0,1:T(8,128)S(1)} fusion(bf16[4096,512]{1,0:T(8,128)(2,1)} %param.12, bf16[512,4096]{1,0:T(8,128)(2,1)} %param.10, f32[4096]{0:T(1024)S(1)} %convert_element_type.64, f32[512]{0:T(512)S(1)} %add_rsqrt_fusion), kind=kOutput, calls=%fused_computation.96 | convolution fusion | flops 2155872256 | bytes 9455616 | tf_op jit(solution)/shard_map/dot_general | solution.py:81
  28.5 31.4 %all-gather.2.cloned.1.call-done = bf16[8192,256]{0,1:T(8,128)(2,1)} async-done(((bf16[512,256]{0,1:T(8,128)(2,1)}), bf16[8192,256]{0,1:T(8,128)(2,1)}) %all-gather.2.cloned.1.call-update) | async-done | bytes 4194320 | tf_op jit(solution)/shard_map/all_gather | solution.py:157
  59.8 6.4 %copy.25 = bf16[8192,256]{1,0:T(8,128)(2,1)} copy(bf16[8192,256]{0,1:T(8,128)(2,1)} %all-gather.2.cloned.1.call-done) | data formatting | bytes 8388608
  66.2 141.5 %while.20 = (s32[]{:T(128)}, f32[4,512]{1,0:T(4,128)S(1)}, f32[4,512]{1,0:T(4,128)S(1)}, f32[4,512,128]{2,1,0:T(8,128)S(1)}, bf16[512,128]{1,0:T(8,128)(2,1)S(1)...) while((s32[]{:T(128)}, f32[4,512]{1,0:T(4,128)S(1)}, ...), condition=%wide.region_9.10_spmd.clone, body=%wide.region_4.9_spmd.clone.sunk | while | flops 617704960 | bytes 17593384 | solution.py:162
  73.5 1.5 fusion.75
  77.8 1.4 fusion.76
  82.3 1.5 fusion.75
  86.7 1.4 fusion.76
  91.2 1.5 fusion.75
  95.5 1.4 fusion.76
  100.0 1.5 fusion.75
  104.3 1.4 fusion.76
  108.9 1.5 fusion.75
  113.2 1.4 fusion.76
  117.7 1.5 fusion.75
  126.6 1.5 fusion.75
  130.9 1.4 fusion.76
  135.4 1.5 fusion.75
  144.3 1.5 fusion.75
  153.1 1.5 fusion.75
  162.0 1.5 fusion.75
  170.8 1.5 fusion.75
  179.6 1.5 fusion.75
  188.5 1.5 fusion.75
  192.8 1.4 fusion.76
  197.3 1.5 fusion.75
  206.2 1.5 fusion.75
  208.2 6.5 %convolution_convert_fusion.1 = bf16[512,4096]{1,0:T(8,128)(2,1)} fusion(bf16[512,512]{0,1:T(8,128)(2,1)S(1)} %bitcast.68, bf16[512,4096]{1,0:T(8,128)(2,1)} %param.15), kind=kOutput, calls=%fused_computation.62 | convolution fusion | flops 2149580800 | bytes 8912896 | tf_op jit(solution)/shard_map/dot_general | solution.py:173
  214.7 84.1 %reduce-scatter.2.cloned.1.call-done = bf16[64,4096]{1,0:T(8,128)(2,1)} async-done(((bf16[512,4096]{1,0:T(8,128)(2,1)}), bf16[64,4096]{1,0:T(8,128)(2,1)}) %reduce-scatter.2.cloned.1.call-update) | async-done | bytes 524304 | tf_op jit(solution)/shard_map/reduce_scatter | solution.py:172
  (256 shorter events, 111.1 us)
Async XLA Ops:
  7.2 4.1 %copy-start.4 = (s32[16]{0:T(128)S(1)}, s32[16]{0:T(128)}, u32[]{:S(2)}) copy-start(s32[16]{0:T(128)} %param.16) | copy-start | bytes 196
  7.2 4.2 %copy-start.3 = (bf16[4096]{0:T(1024)(128)(2,1)S(1)}, bf16[4096]{0:T(1024)(128)(2,1)}, u32[]{:S(2)}) copy-start(bf16[4096]{0:T(1024)(128)(2,1)} %param.11) | copy-start | bytes 24580
  7.2 52.6 %all-gather.2.cloned.1.call-start = ((), (), s32[]{:S(2)}) async-start(), calls=%async_computation.1 | async-start | bytes 4456448 | tf_op jit(solution)/shard_map/all_gather | solution.py:157
  11.4 4.3 %copy-start = (bf16[512,4096]{1,0:T(8,128)(2,1)S(1)}, bf16[512,4096]{1,0:T(8,128)(2,1)}, u32[]{:S(2)}) copy-start(bf16[512,4096]{1,0:T(8,128)(2,1)} %param.10) | copy-start | bytes 12582916
  19.8 279.0 %reduce-scatter.2.cloned.1.call-start = ((), (), s32[]{:S(2)}) async-start(), calls=%async_computation.2 | async-start | bytes 4718592 | tf_op jit(solution)/shard_map/reduce_scatter | solution.py:172
  28.4 37.8 %copy-start.1 = (f32[4,512,128]{2,1,0:T(8,128)S(1)}, f32[4,512,128]{2,1,0:T(8,128)}, u32[]{:S(2)}) copy-start(f32[4,512,128]{2,1,0:T(8,128)} %custom-call.2) | copy-start | bytes 3145732
  28.5 37.8 %copy-start.2 = (s32[64]{0:T(128)S(1)}, s32[64]{0:T(128)}, u32[]{:S(2)}) copy-start(s32[64]{0:T(128)} %param.17) | copy-start | bytes 772
  207.7 7.0 %copy-start.5 = (bf16[512,128]{1,0:T(8,128)(2,1)}, bf16[512,128]{1,0:T(8,128)(2,1)S(1)}, u32[]{:S(2)}) copy-start(bf16[512,128]{1,0:T(8,128)(2,1)S(1)} %get-tuple-element.271) | copy-start | bytes 393220
Sparse Core Ops, SparseCore 0:
  19.9 39.8 all-gather.1
  214.9 83.9 reduce-scatter.1
where the time goes:
time: 308 us; the launch traced here: 306 us
  waiting for transfers between devices  115 us (37%)
  matrix products  81 us (26%)
  other arithmetic  60.7 us (20%)
  local copies, waits for them, and re-layouts  32.6 us (11%)
  between operations  14.3 us (5%)
    reduce_scatter x1, waiting for transfers between devices, on_device(): lax.psum_scatter(jnp.dot(heads_out, w_out, preferred_element_type=jnp.flo...  84.1 us
    all_gather x1, waiting for transfers between devices, on_device(): shard_piece = lax.all_gather(keys_values, 'seq', axis=0, tiled=True)  31.4 us
    dot_general x16, matrix products, attend(): jnp.einsum('hrn,nd->hrd', weights.astype(jnp.bfloat16), value_rows, prefe...  24.5 us
    dot_general x16, matrix products, step_block(): jnp.dot(selector, page_part, preferred_element_type=jnp.float32)  22.8 us
    squeeze x16, local copies, waits for them, and re-layouts, on_device(): lax.scan(step_block, carried, (blocks, block_starts))  15.6 us
    reduce_sum x16, other arithmetic, attend(): running_sum = running_sum * shrink + jnp.sum(weights, axis=2)  14.5 us
    dot_general x16, matrix products, attend(): jnp.einsum('rhd,nd->hrn', group_queries, key_rows, preferred_element_type...  14.2 us
    select_n x16, other arithmetic, step_block(): jnp.where(global_slot // slots_here == seq_rank, global_slot % slots_here...  10.5 us
  transfers between devices with their start and end apart: 2, of which 2 were waited for; matrix products, arithmetic and copies ran while one was open for 3% of the time, Pallas kernels for 0%

commit v1 on v0

--- a/solution.py
+++ b/solution.py
@@ -154,7 +154,9 @@
     )
     initial_cache = jnp.zeros((slots_here * PAGE, cache_width), jnp.bfloat16)
     carried = (initial_states, initial_cache)
-    shard_piece = lax.all_gather(keys_values, "seq", axis=0, tiled=True)
+    shard_piece = jnp.concatenate(
+        lax.all_to_all(jnp.stack([keys_values] * lax.axis_size("seq")), "seq", 0, 0), axis=0
+    )
     piece_rows = shard_piece.shape[0]
     block_rows = 512
     blocks = shard_piece.reshape(piece_rows // block_rows, block_rows, 2 * HD)

time: 308 us -> 318 us (1.032)
  waiting for transfers between devices: 115 us -> 126 us
  starting transfers between devices: 0.26 us -> 5.86 us
  local copies, waits for them, and re-layouts: 32.6 us -> 28.8 us
    all_to_all x0 -> x1, waiting for transfers between devices: none -> 41.8 us  [on_device(): lax.all_to_all(jnp.stack([keys_values] * lax.axis_size('seq')), 'seq', 0, 0)]
    all_gather x1 -> x0, waiting for transfers between devices: 31.4 us -> none  [on_device(): shard_piece = lax.all_gather(keys_values, 'seq', axis=0, tiled=True)]
    unnamed x15 -> x14, local copies, waits for them, and re-layouts: 7.11 us -> 0.7 us
    all_to_all x0 -> x1, starting transfers between devices: none -> 5.64 us  [on_device(): lax.all_to_all(jnp.stack([keys_values] * lax.axis_size('seq')), 'seq', 0, 0)]
where the time goes in v1:
time: 318 us; the launch traced here: 316 us
  waiting for transfers between devices  126 us (40%)
  matrix products  81.1 us (26%)
  other arithmetic  58.7 us (18%)
  local copies, waits for them, and re-layouts  28.8 us (9%)
  between operations  14.3 us (4%)
  starting transfers between devices  5.86 us (2%)
    reduce_scatter x1, waiting for transfers between devices, on_device(): lax.psum_scatter(jnp.dot(heads_out, w_out, preferred_element_type=jnp.flo...  84.5 us
    all_to_all x1, waiting for transfers between devices, on_device(): lax.all_to_all(jnp.stack([keys_values] * lax.axis_size('seq')), 'seq', 0, 0)  41.8 us
    dot_general x16, matrix products, attend(): jnp.einsum('hrn,nd->hrd', weights.astype(jnp.bfloat16), value_rows, prefe...  24.5 us
    dot_general x16, matrix products, step_block(): jnp.dot(selector, page_part, preferred_element_type=jnp.float32)  22.8 us
    squeeze x16, local copies, waits for them, and re-layouts, on_device(): lax.scan(step_block, carried, (blocks, block_starts))  15.6 us
    reduce_sum x16, other arithmetic, attend(): running_sum = running_sum * shrink + jnp.sum(weights, axis=2)  14.5 us
    dot_general x16, matrix products, attend(): jnp.einsum('rhd,nd->hrn', group_queries, key_rows, preferred_element_type...  14.3 us
    select_n x16, other arithmetic, step_block(): jnp.where(global_slot // slots_here == seq_rank, global_slot % slots_here...  10 us
  transfers between devices with their start and end apart: 2, of which 2 were waited for; matrix products, arithmetic and copies ran while one was open for 3% of the time, Pallas kernels for 0%

profile of v1, /device:TPU:0, one launch (start us, length us, event | category | flops | bytes accessed | tf_op | source)
XLA Modules:
  0.0 316.4 jit_solution(9558670382999147603)
XLA Ops:
  8.1 3.1 fusion.33
  11.3 4.2 %convolution_convert_fusion.2 = bf16[512,128]{0,1:T(8,128)(2,1)S(1)} fusion(bf16[4096,512]{1,0:T(8,128)(2,1)} %param.14, s32[]{:T(128)S(6)} %select_n.116, bf16[512,4096]{1,0:T(8,128)(2,1)} %param.10, f32[4096]{0:T(1024)S(1)} %convert_element_type.64, f32[512]{0:T(512)S(1)} %add_rsqrt_fusion), kind=kOutput, calls=%fused_computation.64 | convolution fusion | flops 545325056 | bytes 5392388 | tf_op jit(solution)/shard_map/dot_general | solution.py:91
  15.6 2.8 convolution_bitcast_fusion
  19.2 2.4 stack.2
  21.6 5.6 %all-to-all-start = ((bf16[16,512,256]{2,1,0:T(8,128)(2,1)}), bf16[16,512,256]{2,1,0:T(8,128)(2,1)}, u32[]{:S(2)}, u32[]{:S(2)}) async-start(bf16[16,512,256]{2,1,0:T(8,128)(2,1)} %stack.2), calls=%async_computation | async-start | bytes 8388608 | tf_op jit(solution)/shard_map/all_to_all | solution.py:158
  27.5 5.9 %fusion.50 = f32[512,512]{0,1:T(8,128)S(1)} fusion(bf16[4096,512]{1,0:T(8,128)(2,1)} %param.12, bf16[512,4096]{1,0:T(8,128)(2,1)} %param.10, f32[4096]{0:T(1024)S(1)} %convert_element_type.64, f32[512]{0:T(512)S(1)} %add_rsqrt_fusion), kind=kOutput, calls=%fused_computation.96 | convolution fusion | flops 2155872256 | bytes 9455616 | tf_op jit(solution)/shard_map/dot_general | solution.py:81
  35.8 41.8 %all-to-all-done = bf16[16,512,256]{2,1,0:T(8,128)(2,1)} async-done(((bf16[16,512,256]{2,1,0:T(8,128)(2,1)}), bf16[16,512,256]{2,1,0:T(8,128)(2,1)}, u32[]{:S(2)}, u32[]{:S(2)}) %all-to-all-start) | async-done | bytes 4194336 | tf_op jit(solution)/shard_map/all_to_all | solution.py:158
  77.6 140.4 %while.20 = (s32[]{:T(128)}, f32[4,512]{1,0:T(4,128)S(1)}, f32[4,512]{1,0:T(4,128)S(1)}, f32[4,512,128]{2,1,0:T(8,128)S(1)}, bf16[512,128]{1,0:T(8,128)(2,1)S(1)...) while((s32[]{:T(128)}, f32[4,512]{1,0:T(4,128)S(1)}, ...), condition=%wide.region_9.10_spmd.clone, body=%wide.region_4.9_spmd.clone.sunk | while | flops 617704960 | bytes 17593384 | solution.py:164
  84.8 1.5 fusion.75
  93.6 1.5 fusion.75
  97.9 1.4 fusion.76
  102.4 1.5 fusion.75
  111.2 1.5 fusion.75
  115.4 1.4 fusion.76
  120.0 1.5 fusion.75
  128.7 1.5 fusion.75
  133.0 1.4 fusion.76
  137.5 1.5 fusion.75
  146.3 1.5 fusion.75
  150.5 1.4 fusion.76
  155.1 1.5 fusion.75
  163.8 1.5 fusion.75
  168.1 1.4 fusion.76
  172.6 1.5 fusion.75
  181.4 1.5 fusion.75
  185.6 1.4 fusion.76
  190.2 1.5 fusion.75
  199.0 1.5 fusion.75
  207.7 1.5 fusion.75
  216.5 1.5 fusion.75
  218.6 6.5 %convolution_convert_fusion.1 = bf16[512,4096]{1,0:T(8,128)(2,1)} fusion(bf16[512,512]{0,1:T(8,128)(2,1)S(1)} %bitcast.66, bf16[512,4096]{1,0:T(8,128)(2,1)} %param.15), kind=kOutput, calls=%fused_computation.62 | convolution fusion | flops 2149580800 | bytes 8912896 | tf_op jit(solution)/shard_map/dot_general | solution.py:175
  225.1 84.5 %reduce-scatter.2.cloned.1.call-done = bf16[64,4096]{1,0:T(8,128)(2,1)} async-done(((bf16[512,4096]{1,0:T(8,128)(2,1)}), bf16[64,4096]{1,0:T(8,128)(2,1)}) %reduce-scatter.2.cloned.1.call-update) | async-done | bytes 524304 | tf_op jit(solution)/shard_map/reduce_scatter | solution.py:174
  (256 shorter events, 110.8 us)
Async XLA Ops:
  7.2 4.0 %copy-start.4 = (s32[16]{0:T(128)S(1)}, s32[16]{0:T(128)}, u32[]{:S(2)}) copy-start(s32[16]{0:T(128)} %param.16) | copy-start | bytes 196
  7.2 4.1 %copy-start.3 = (bf16[4096]{0:T(1024)(128)(2,1)S(1)}, bf16[4096]{0:T(1024)(128)(2,1)}, u32[]{:S(2)}) copy-start(bf16[4096]{0:T(1024)(128)(2,1)} %param.11) | copy-start | bytes 24580
  11.3 4.3 %copy-start = (bf16[512,4096]{1,0:T(8,128)(2,1)S(1)}, bf16[512,4096]{1,0:T(8,128)(2,1)}, u32[]{:S(2)}) copy-start(bf16[512,4096]{1,0:T(8,128)(2,1)} %param.10) | copy-start | bytes 12582916
  21.6 56.0 %all-to-all-start = ((bf16[16,512,256]{2,1,0:T(8,128)(2,1)}), bf16[16,512,256]{2,1,0:T(8,128)(2,1)}, u32[]{:S(2)}, u32[]{:S(2)}) async-start(bf16[16,512,256]{2,1,0:T(8,128)(2,1)} %stack.2), calls=%async_computation | async-start | bytes 8388608 | tf_op jit(solution)/shard_map/all_to_all | solution.py:158
  27.2 282.4 %reduce-scatter.2.cloned.1.call-start = ((), (), s32[]{:S(2)}) async-start(), calls=%async_computation.2 | async-start | bytes 4718592 | tf_op jit(solution)/shard_map/reduce_scatter | solution.py:174
  33.6 44.1 %copy-start.2 = (s32[64]{0:T(128)S(1)}, s32[64]{0:T(128)}, u32[]{:S(2)}) copy-start(s32[64]{0:T(128)} %param.17) | copy-start | bytes 772
  34.3 43.4 %copy-start.1 = (f32[4,512,128]{2,1,0:T(8,128)S(1)}, f32[4,512,128]{2,1,0:T(8,128)}, u32[]{:S(2)}) copy-start(f32[4,512,128]{2,1,0:T(8,128)} %custom-call.2) | copy-start | bytes 3145732
  218.1 7.0 %copy-start.5 = (bf16[512,128]{1,0:T(8,128)(2,1)}, bf16[512,128]{1,0:T(8,128)(2,1)S(1)}, u32[]{:S(2)}) copy-start(bf16[512,128]{1,0:T(8,128)(2,1)S(1)} %get-tuple-element.271) | copy-start | bytes 393220
Sparse Core Ops, SparseCore 0:
  225.2 84.3 reduce-scatter.1
